TPU v7x, 256 devices: a whole 4x4x8 slice. The times are simulated.
256 devices in a mesh: seq: 32 (over z, y_hi, core), tp: 8 (over y_lo, x).
Axes of the slice: x: 4, y: 4 (y_hi: 2, y_lo: 2; y = y_hi * 2 + y_lo), z: 8, core: 2. Of those that a mesh axis runs over, the one named last changes fastest.
Arguments:
- queries: bfloat16 [12288, 3072], P('seq', 'tp'), may hold values from -16 to 16
- keys: bfloat16 [12288, 3072], P('seq', 'tp'), may hold values from -6 to 6
- values: bfloat16 [12288, 3072], P('seq', 'tp'), may hold values from -6 to 6
- resid: bfloat16 [12288, 6144], P(('seq', 'tp')), may hold values from -6 to 6
- out_weight: bfloat16 [3072, 6144], P('tp'), may hold values from -0.109375 to 0.109375
- gain: float32 [6144], replicated, may hold values from 0.1 to 1.9
- pair_of_device: int32 [32], replicated, may hold values from 0 to 31, each once
- frame_of_tile: int32 [64], replicated, may hold values from 0 to 8, as said below
Outputs:
- layer_out: bfloat16 [12288, 6144], P(('seq', 'tp'))
Inputs may be any that keep to these rules, and one draw needn't show every extreme that they name: `pair_of_device`: each value once. Frames have equal length, 8 tiles; the sequence starts inside frame 0 and ends inside frame 8, so only these two are partial: frame_of_tile[t] = (t + o) // 8 for an offset o from 1 to 7.
All inputs are finite; a program needn't handle non-finite values.
Results may differ from a plain program's by a relative error of at most 0.025.
Values may be sent and summed in bfloat16 or wider, within the bound.
No kernel may reach another device: no remote copies, remote signals or barrier semaphores. Data moves between devices by JAX's collectives and lax.ppermute only.
A program may use at most 128 MiB of HBM per device.

v0:
```python
import math
import jax
import jax.numpy as jnp
from jax import lax
from jax.sharding import PartitionSpec as P

HEAD = 128


def slot_frames(pair_of_device, frame_of_tile, tile_count):
    slot_ids = jnp.arange(tile_count, dtype=jnp.int32)
    paired = jnp.repeat(pair_of_device, 2)
    tile_ids = jnp.where(slot_ids % 2 == 0, paired, tile_count - 1 - paired)
    matches = tile_ids[:, None] == jnp.arange(tile_count, dtype=jnp.int32)[None, :]
    return jnp.sum(jnp.where(matches, frame_of_tile[None, :], 0), axis=1)


def frames_of_rows(slot_frame, offset, row_count, span_rows):
    row_slots = (offset + jnp.arange(row_count, dtype=jnp.int32)) // span_rows
    matches = row_slots[:, None] == jnp.arange(slot_frame.shape[0], dtype=jnp.int32)[None, :]
    return jnp.sum(jnp.where(matches, slot_frame[None, :], 0), axis=1)


def softmax_update(carry_state, query_heads, query_frame, key_rows, value_rows, key_frame):
    head_count = query_heads.shape[1]
    key_heads = key_rows.reshape(key_rows.shape[0], head_count, HEAD)
    value_heads = value_rows.reshape(value_rows.shape[0], head_count, HEAD)
    allowed = (key_frame[None, :] <= query_frame[:, None])[None, :, :]
    score_scale = 1.0 / math.sqrt(HEAD)
    run_max, run_totals, weighted = carry_state
    scores = (
        jnp.einsum("qhd,khd->hqk", query_heads, key_heads, preferred_element_type=jnp.float32)
        * score_scale
    )
    masked = jnp.where(allowed, scores, jnp.float32(-1e30))
    new_max = jnp.maximum(run_max, jnp.max(masked, axis=-1))
    probs = jnp.where(allowed, jnp.exp(masked - new_max[..., None]), jnp.float32(0.0))
    rescale = jnp.exp(run_max - new_max)
    new_totals = run_totals * rescale + jnp.sum(probs, axis=-1)
    product = jnp.einsum(
        "hqk,khd->hqd", probs.astype(jnp.bfloat16), value_heads, preferred_element_type=jnp.float32
    )
    return (new_max, new_totals, weighted * rescale[..., None] + product)


def empty_state(head_count, row_count):
    return (
        jnp.full((head_count, row_count), -1e30, jnp.float32),
        jnp.zeros((head_count, row_count), jnp.float32),
        jnp.zeros((head_count, row_count, HEAD), jnp.float32),
    )


def local(queries, keys, values, resid, out_weight, gain, pair_of_device, frame_of_tile):
    tok_rows, row_width = queries.shape
    head_count = row_width // HEAD
    span_rows = tok_rows // 2
    seq_count = lax.axis_size("seq")
    seq_index = lax.axis_index("seq")
    slot_frame = slot_frames(pair_of_device, frame_of_tile, 2 * seq_count)
    own_frames = lax.dynamic_slice_in_dim(slot_frame, 2 * seq_index, 2, 0)
    row_frame = jnp.repeat(own_frames, span_rows)
    query_heads = queries.reshape(tok_rows, head_count, HEAD)
    key_rows = lax.all_gather(keys, "seq", axis=0, tiled=True)
    value_rows = lax.all_gather(values, "seq", axis=0, tiled=True)
    key_count = key_rows.shape[0]
    key_blocks = key_rows.reshape(key_count // 512, 512, row_width)
    value_blocks = value_rows.reshape(key_count // 512, 512, row_width)

    def advance(inner_state, entry):
        key_block, value_block, block_index = entry
        key_frame = frames_of_rows(slot_frame, block_index * 512, 512, span_rows)
        return (
            softmax_update(inner_state, query_heads, row_frame, key_block, value_block, key_frame),
            None,
        )

    final_state, unused = lax.scan(
        advance,
        empty_state(head_count, tok_rows),
        (key_blocks, value_blocks, jnp.arange(key_count // 512, dtype=jnp.int32)),
    )
    run_max, run_totals, weighted = final_state
    attn_heads = jnp.transpose(weighted / run_totals[..., None], (1, 0, 2))
    attn = attn_heads.reshape(tok_rows, row_width).astype(jnp.bfloat16)
    branch = lax.psum_scatter(
        jnp.dot(attn, out_weight, preferred_element_type=jnp.float32).astype(jnp.bfloat16),
        "tp",
        scatter_dimension=0,
        tiled=True,
    ).astype(jnp.float32)
    rms = jnp.sqrt(jnp.mean(branch * branch, axis=-1) + 1e-06)
    layer_out = resid.astype(jnp.float32) + gain[None, :] * branch / rms[:, None]
    return layer_out.astype(jnp.bfloat16)


def solution(mesh):
    in_specs = (
        P("seq", "tp"),
        P("seq", "tp"),
        P("seq", "tp"),
        P(("seq", "tp"), None),
        P("tp", None),
        P(),
        P(),
        P(),
    )
    out_specs = P(("seq", "tp"), None)
    return jax.shard_map(local, mesh=mesh, in_specs=in_specs, out_specs=out_specs, check_vma=False)
```

profile of v0, /device:TPU:1, one launch (start us, length us, event | category | flops | bytes accessed | tf_op | source)
XLA Modules:
  0.0 436.5 jit_solution(12909804964037090042)
XLA Ops:
  6.5 0.7 all-gather.3.cloned.1.call-update
  7.3 0.7 all-gather.5.cloned.1.call-update
  8.1 0.7 broadcast_in_dim.89
  8.9 1.2 copy.27
  10.3 0.8 select_reduce_fusion.1
  11.2 108.5 %all-gather.3.cloned.1.call-done = bf16[12288,384]{1,0:T(8,128)(2,1)} async-done(((bf16[384,384]{1,0:T(8,128)(2,1)}), bf16[12288,384]{1,0:T(8,128)(2,1)}) %all-gather.3.cloned.1.call-update) | async-done | bytes 9437200 | tf_op jit(solution)/shard_map/all_gather | solution.py:64
  119.8 104.7 %all-gather.5.cloned.1.call-done = bf16[12288,384]{1,0:T(8,128)(2,1)} async-done(((bf16[384,384]{1,0:T(8,128)(2,1)}), bf16[12288,384]{1,0:T(8,128)(2,1)}) %all-gather.5.cloned.1.call-update) | async-done | bytes 9437200 | tf_op jit(solution)/shard_map/all_gather | solution.py:65
  224.5 137.8 %while.17 = (s32[]{:T(128)}, f32[3,384]{1,0:T(4,128)S(1)}, f32[3,384]{1,0:T(4,128)S(1)}, f32[3,384,128]{2,1,0:T(8,128)S(1)}, s32[24]{0:T(128)S(1)}, /*index=5*/s...) while((s32[]{:T(128)}, f32[3,384]{1,0:T(4,128)S(1)}, ...), condition=%wide.region_5.6_spmd.clone, body=%wide.region_1.5_spmd.clone.sunk | while | flops 310404736 | bytes 13359545 | solution.py:78
  226.1 1.2 constant_dynamic-slice_fusion.3
  229.1 1.1 convolution_add_fusion.2
  231.9 1.2 constant_dynamic-slice_fusion.3
  233.5 0.7 fusion.35
  234.8 1.1 convolution_add_fusion.2
  237.6 1.2 constant_dynamic-slice_fusion.3
  239.2 0.7 fusion.35
  240.6 1.1 convolution_add_fusion.2
  243.4 1.2 constant_dynamic-slice_fusion.3
  245.0 0.7 fusion.35
  246.3 1.1 convolution_add_fusion.2
  249.1 1.2 constant_dynamic-slice_fusion.3
  250.7 0.7 fusion.35
  252.1 1.1 convolution_add_fusion.2
  254.9 1.2 constant_dynamic-slice_fusion.3
  257.8 1.1 convolution_add_fusion.2
  260.6 1.2 constant_dynamic-slice_fusion.3
  263.6 1.1 convolution_add_fusion.2
  266.3 1.2 constant_dynamic-slice_fusion.3
  269.3 1.1 convolution_add_fusion.2
  272.1 1.2 constant_dynamic-slice_fusion.3
  275.0 1.1 convolution_add_fusion.2
  277.8 1.2 constant_dynamic-slice_fusion.3
  280.8 1.1 convolution_add_fusion.2
  283.6 1.2 constant_dynamic-slice_fusion.3
  286.5 1.1 convolution_add_fusion.2
  289.3 1.2 constant_dynamic-slice_fusion.3
  292.3 1.1 convolution_add_fusion.2
  295.1 1.2 constant_dynamic-slice_fusion.3
  298.0 1.1 convolution_add_fusion.2
  300.8 1.2 constant_dynamic-slice_fusion.3
  303.8 1.1 convolution_add_fusion.2
  306.5 1.2 constant_dynamic-slice_fusion.3
  309.5 1.1 convolution_add_fusion.2
  312.3 1.2 constant_dynamic-slice_fusion.3
  315.2 1.1 convolution_add_fusion.2
  318.0 1.2 constant_dynamic-slice_fusion.3
  321.0 1.1 convolution_add_fusion.2
  323.8 1.2 constant_dynamic-slice_fusion.3
  326.7 1.1 convolution_add_fusion.2
  329.5 1.2 constant_dynamic-slice_fusion.3
  332.5 1.1 convolution_add_fusion.2
  335.3 1.2 constant_dynamic-slice_fusion.3
  338.2 1.1 convolution_add_fusion.2
  341.0 1.2 constant_dynamic-slice_fusion.3
  344.0 1.1 convolution_add_fusion.2
  346.7 1.2 constant_dynamic-slice_fusion.3
  349.7 1.1 convolution_add_fusion.2
  352.5 1.2 constant_dynamic-slice_fusion.3
  355.4 1.1 convolution_add_fusion.2
  358.2 1.2 constant_dynamic-slice_fusion.3
  361.2 1.1 convolution_add_fusion.2
  362.6 7.1 %convolution_convert_fusion = bf16[384,6144]{1,0:T(8,128)(2,1)} fusion(bf16[384,384]{0,1:T(8,128)(2,1)S(1)} %bitcast.45, bf16[384,6144]{1,0:T(8,128)(2,1)} %param.14), kind=kOutput, calls=%fused_computation.29 | convolution fusion | flops 1814298624 | bytes 9732096 | tf_op jit(solution)/shard_map/dot_general | solution.py:87
  369.7 56.8 %reduce-scatter.2.cloned.1.call-done = bf16[48,6144]{1,0:T(8,128)(2,1)} async-done(((bf16[384,6144]{1,0:T(8,128)(2,1)}), bf16[48,6144]{1,0:T(8,128)(2,1)}) %reduce-scatter.2.cloned.1.call-update) | async-done | bytes 589840 | tf_op jit(solution)/shard_map/reduce_scatter | solution.py:86
  426.5 1.3 fusion.18
  427.8 2.1 fusion.17
  (327 shorter events, 64.8 us)
Async XLA Ops:
  6.5 113.2 %all-gather.3.cloned.1.call-start = ((), (), s32[]{:S(2)}) async-start(), calls=%async_computation.1 | async-start | bytes 9732096 | tf_op jit(solution)/shard_map/all_gather | solution.py:64
  7.3 217.2 %all-gather.5.cloned.1.call-start = ((), (), s32[]{:S(2)}) async-start(), calls=%async_computation.2 | async-start | bytes 9732096 | tf_op jit(solution)/shard_map/all_gather | solution.py:65
  8.0 418.5 %reduce-scatter.2.cloned.1.call-start = ((), (), s32[]{:S(2)}) async-start(), calls=%async_computation.3 | async-start | bytes 5308416 | tf_op jit(solution)/shard_map/reduce_scatter | solution.py:86
  369.7 58.1 %copy-start = (bf16[48,6144]{1,0:T(8,128)(2,1)S(1)}, bf16[48,6144]{1,0:T(8,128)(2,1)}, u32[]{:S(2)}) copy-start(bf16[48,6144]{1,0:T(8,128)(2,1)} %param.13) | copy-start | bytes 1769476
  369.7 58.1 %copy-start.1 = (f32[6144]{0:T(1024)S(1)}, f32[6144]{0:T(1024)}, u32[]{:S(2)}) copy-start(f32[6144]{0:T(1024)} %param.15) | copy-start | bytes 73732
Sparse Core Ops, SparseCore 0:
  10.1 109.5 all-gather.2
  122.5 101.8 all-gather.4
  369.8 56.6 reduce-scatter.1
where the time goes:
time: 437 us; the launch traced here: 436 us
  waiting for transfers between devices  271 us (62%)
  local copies, waits for them, and re-layouts  59.5 us (14%)
  matrix products  49.3 us (11%)
  other arithmetic  26.6 us (6%)
  loops' own time  16.4 us (4%)
  between operations  13.2 us (3%)
    all_gather x1, waiting for transfers between devices, local(): key_rows = lax.all_gather(keys, 'seq', axis=0, tiled=True)  109 us
    all_gather x1, waiting for transfers between devices, local(): value_rows = lax.all_gather(values, 'seq', axis=0, tiled=True)  105 us
    reduce_scatter x1, waiting for transfers between devices, local(): lax.psum_scatter(jnp.dot(attn, out_weight, preferred_element_type=jnp.flo...  56.8 us
    dynamic_slice x96, local copies, waits for them, and re-layouts, local(): lax.scan(advance, empty_state(head_count, tok_rows), (key_blocks, value_b...  53.2 us
    dot_general x24, matrix products, softmax_update(): jnp.einsum('hqk,khd->hqd', probs.astype(jnp.bfloat16), value_heads, prefe...  25.8 us
    another operation x1, loops' own time, local(): lax.scan(advance, empty_state(head_count, tok_rows), (key_blocks, value_b...  16.4 us
    dot_general x24, matrix products, softmax_update(): jnp.einsum('qhd,khd->hqk', query_heads, key_heads, preferred_element_type...  16.3 us
    reduce_sum x24, other arithmetic, softmax_update(): new_totals = run_totals * rescale + jnp.sum(probs, axis=-1)  14.9 us
  transfers between devices with their start and end apart: 3, of which 3 were waited for; matrix products, arithmetic and copies ran while one was open for 1% of the time, Pallas kernels for 0%

commit v1 on v0

--- a/solution.py
+++ b/solution.py
@@ -61,7 +61,9 @@
     own_frames = lax.dynamic_slice_in_dim(slot_frame, 2 * seq_index, 2, 0)
     row_frame = jnp.repeat(own_frames, span_rows)
     query_heads = queries.reshape(tok_rows, head_count, HEAD)
-    key_rows = lax.all_gather(keys, "seq", axis=0, tiled=True)
+    key_rows = jnp.concatenate(
+        lax.all_to_all(jnp.stack([keys] * lax.axis_size("seq")), "seq", 0, 0), axis=0
+    )
     value_rows = lax.all_gather(values, "seq", axis=0, tiled=True)
     key_count = key_rows.shape[0]
     key_blocks = key_rows.reshape(key_count // 512, 512, row_width)

time: 437 us -> 548 us (1.25)
  matrix products: 49.3 us -> 114 us
  waiting for transfers between devices: 271 us -> 298 us
  starting transfers between devices: 0.08 us -> 13 us
  local copies, waits for them, and re-layouts: 59.5 us -> 65.2 us
    all_to_all x0 -> x1, waiting for transfers between devices: none -> 235 us  [local(): lax.all_to_all(jnp.stack([keys] * lax.axis_size('seq')), 'seq', 0, 0)]
    all_gather x1 -> x0, waiting for transfers between devices: 109 us -> none  [local(): key_rows = lax.all_gather(keys, 'seq', axis=0, tiled=True)]
    all_gather x1, waiting for transfers between devices: 105 us -> 0.01 us  [local(): value_rows = lax.all_gather(values, 'seq', axis=0, tiled=True)]
    dot_general x24, matrix products: 25.8 us -> 67.5 us  [softmax_update(): jnp.einsum('hqk,khd->hqd', probs.astype(jnp.bfloat16), value_heads, prefe...]
    dot_general x24, matrix products: 16.3 us -> 39.3 us  [softmax_update(): jnp.einsum('qhd,khd->hqk', query_heads, key_heads, preferred_element_type...]
    all_to_all x0 -> x1, starting transfers between devices: none -> 12.9 us  [local(): lax.all_to_all(jnp.stack([keys] * lax.axis_size('seq')), 'seq', 0, 0)]
    another operation x0 -> x1, local copies, waits for them, and re-layouts: none -> 6.1 us  [local(): jnp.stack([keys] * lax.axis_size('seq'))]
  transfers between devices with their start and end apart: 3 -> 3, of which waited for: 3 -> 2; matrix products, arithmetic and copies ran while one was open for 1% -> 0% of each run, Pallas kernels for 0% -> 0%
where the time goes in v1:
time: 548 us; the launch traced here: 545 us
  waiting for transfers between devices  298 us (54%)
  matrix products  114 us (21%)
  local copies, waits for them, and re-layouts  65.2 us (12%)
  other arithmetic  25.7 us (5%)
  loops' own time  16 us (3%)
  between operations  13.5 us (2%)
  starting transfers between devices  13 us (2%)
    all_to_all x1, waiting for transfers between devices, local(): lax.all_to_all(jnp.stack([keys] * lax.axis_size('seq')), 'seq', 0, 0)  235 us
    dot_general x24, matrix products, softmax_update(): jnp.einsum('hqk,khd->hqd', probs.astype(jnp.bfloat16), value_heads, prefe...  67.5 us
    reduce_scatter x1, waiting for transfers between devices, local(): lax.psum_scatter(jnp.dot(attn, out_weight, preferred_element_type=jnp.flo...  61.5 us
    dynamic_slice x96, local copies, waits for them, and re-layouts, local(): lax.scan(advance, empty_state(head_count, tok_rows), (key_blocks, value_b...  52.7 us
    dot_general x24, matrix products, softmax_update(): jnp.einsum('qhd,khd->hqk', query_heads, key_heads, preferred_element_type...  39.3 us
    another operation x1, loops' own time, local(): lax.scan(advance, empty_state(head_count, tok_rows), (key_blocks, value_b...  16 us
    reduce_sum x24, other arithmetic, softmax_update(): new_totals = run_totals * rescale + jnp.sum(probs, axis=-1)  14.7 us
    all_to_all x1, starting transfers between devices, local(): lax.all_to_all(jnp.stack([keys] * lax.axis_size('seq')), 'seq', 0, 0)  12.9 us
  transfers between devices with their start and end apart: 3, of which 2 were waited for; matrix products, arithmetic and copies ran while one was open for 0% of the time, Pallas kernels for 0%

profile of v1, /device:TPU:1, one launch (start us, length us, event | category | flops | bytes accessed | tf_op | source)
XLA Modules:
  0.0 544.9 jit_solution(14347014139067150650)
XLA Ops:
  6.5 6.1 %stack.2 = bf16[32,384,384]{2,1,0:T(8,128)(2,1)} broadcast(bf16[384,384]{1,0:T(8,128)(2,1)} %param.11), dimensions={1,2} | broadcast | bytes 9732096 | tf_op jit(solution)/shard_map/stack | solution.py:65
  12.6 12.9 %all-to-all-start = ((bf16[32,384,384]{2,1,0:T(8,128)(2,1)}), bf16[32,384,384]{2,1,0:T(8,128)(2,1)}, u32[]{:S(2)}, u32[]{:S(2)}) async-start(bf16[32,384,384]{2,1,0:T(8,128)(2,1)} %stack.2), calls=%async_computation | async-start | bytes 18874368 | tf_op jit(solution)/shard_map/all_to_all | solution.py:65
  28.0 235.4 %all-to-all-done = bf16[32,384,384]{2,1,0:T(8,128)(2,1)} async-done(((bf16[32,384,384]{2,1,0:T(8,128)(2,1)}), bf16[32,384,384]{2,1,0:T(8,128)(2,1)}, u32[]{:S(2)}, u32[]{:S(2)}) %all-to-all-start) | async-done | bytes 9437216 | tf_op jit(solution)/shard_map/all_to_all | solution.py:65
  263.4 201.3 %while.17 = (s32[]{:T(128)}, f32[3,384]{1,0:T(4,128)S(1)}, f32[3,384]{1,0:T(4,128)S(1)}, f32[3,384,128]{2,1,0:T(8,128)}, s32[24]{0:T(128)S(1)}, /*index=5*/s32[6...) while((s32[]{:T(128)}, f32[3,384]{1,0:T(4,128)S(1)}, ...), condition=%wide.region_5.6_spmd.clone, body=%wide.region_1.5_spmd.clone.sunk | while | flops 310404736 | bytes 13359537 | solution.py:80
  265.0 1.2 constant_dynamic-slice_fusion.3
  266.4 1.6 fusion.35
  268.9 1.8 convolution_add_fusion.2
  272.4 1.2 constant_dynamic-slice_fusion.3
  273.8 1.6 fusion.35
  276.3 2.9 convolution_add_fusion.2
  280.8 1.2 constant_dynamic-slice_fusion.3
  282.2 1.6 fusion.35
  284.7 2.9 convolution_add_fusion.2
  289.3 1.2 constant_dynamic-slice_fusion.3
  290.7 1.6 fusion.35
  293.2 2.9 convolution_add_fusion.2
  299.1 1.6 fusion.35
  301.6 2.9 convolution_add_fusion.2
  306.1 1.2 constant_dynamic-slice_fusion.3
  307.5 1.6 fusion.35
  310.0 2.9 convolution_add_fusion.2
  314.6 1.2 constant_dynamic-slice_fusion.3
  316.0 1.6 fusion.35
  318.5 2.9 convolution_add_fusion.2
  323.0 1.2 constant_dynamic-slice_fusion.3
  324.4 1.6 fusion.35
  326.9 2.9 convolution_add_fusion.2
  332.8 1.6 fusion.35
  335.3 2.9 convolution_add_fusion.2
  341.3 1.6 fusion.35
  343.7 2.9 convolution_add_fusion.2
  349.7 1.6 fusion.35
  352.2 2.9 convolution_add_fusion.2
  358.1 1.6 fusion.35
  360.6 2.9 convolution_add_fusion.2
  366.5 1.6 fusion.35
  369.0 2.9 convolution_add_fusion.2
  375.0 1.6 fusion.35
  377.5 2.9 convolution_add_fusion.2
  383.4 1.6 fusion.35
  385.9 2.9 convolution_add_fusion.2
  391.8 1.6 fusion.35
  394.3 2.9 convolution_add_fusion.2
  400.3 1.6 fusion.35
  402.7 2.9 convolution_add_fusion.2
  408.7 1.6 fusion.35
  411.2 2.9 convolution_add_fusion.2
  417.1 1.6 fusion.35
  419.6 2.9 convolution_add_fusion.2
  425.5 1.6 fusion.35
  428.0 2.9 convolution_add_fusion.2
  434.0 1.6 fusion.35
  436.5 2.9 convolution_add_fusion.2
  442.4 1.6 fusion.35
  444.9 2.9 convolution_add_fusion.2
  450.8 1.6 fusion.35
  453.3 2.9 convolution_add_fusion.2
  459.3 1.6 fusion.35
  461.8 2.9 convolution_add_fusion.2
  464.6 1.3 copy.31
  466.0 7.1 %convolution_convert_fusion = bf16[384,6144]{1,0:T(8,128)(2,1)} fusion(bf16[384,384]{0,1:T(8,128)(2,1)S(1)} %bitcast.45, bf16[384,6144]{1,0:T(8,128)(2,1)} %param.14), kind=kOutput, calls=%fused_computation.29 | convolution fusion | flops 1814298624 | bytes 9732096 | tf_op jit(solution)/shard_map/dot_general | solution.py:89
  473.1 61.5 %reduce-scatter.2.cloned.1.call-done = bf16[48,6144]{1,0:T(8,128)(2,1)} async-done(((bf16[384,6144]{1,0:T(8,128)(2,1)}), bf16[48,6144]{1,0:T(8,128)(2,1)}) %reduce-scatter.2.cloned.1.call-update) | async-done | bytes 589840 | tf_op jit(solution)/shard_map/reduce_scatter | solution.py:88
  534.6 1.3 fusion.18
  535.9 2.1 fusion.17
  (333 shorter events, 72.5 us)
Async XLA Ops:
  12.6 13.8 %copy-start.3 = (s32[32]{0:T(128)S(1)}, s32[32]{0:T(128)}, u32[]{:S(2)}) copy-start(s32[32]{0:T(128)} %param.16) | copy-start | bytes 388
  12.6 14.0 %copy-start.1 = (bf16[384,384]{1,0:T(8,128)(2,1)S(1)}, bf16[384,384]{1,0:T(8,128)(2,1)}, u32[]{:S(2)}) copy-start(bf16[384,384]{1,0:T(8,128)(2,1)} %param.10) | copy-start | bytes 884740
  12.6 15.1 %copy-start.4 = (s32[64]{0:T(128)S(1)}, s32[64]{0:T(128)}, u32[]{:S(2)}) copy-start(s32[64]{0:T(128)} %param.17) | copy-start | bytes 772
  12.6 250.7 %all-to-all-start = ((bf16[32,384,384]{2,1,0:T(8,128)(2,1)}), bf16[32,384,384]{2,1,0:T(8,128)(2,1)}, u32[]{:S(2)}, u32[]{:S(2)}) async-start(bf16[32,384,384]{2,1,0:T(8,128)(2,1)} %stack.2), calls=%async_computation | async-start | bytes 18874368 | tf_op jit(solution)/shard_map/all_to_all | solution.py:65
  25.6 237.8 %all-gather.2.cloned.1.call-start = ((), (), s32[]{:S(2)}) async-start(), calls=%async_computation.2 | async-start | bytes 9732096 | tf_op jit(solution)/shard_map/all_gather | solution.py:67
  26.3 508.3 %reduce-scatter.2.cloned.1.call-start = ((), (), s32[]{:S(2)}) async-start(), calls=%async_computation.3 | async-start | bytes 5308416 | tf_op jit(solution)/shard_map/reduce_scatter | solution.py:88
  473.1 62.8 %copy-start = (bf16[48,6144]{1,0:T(8,128)(2,1)S(1)}, bf16[48,6144]{1,0:T(8,128)(2,1)}, u32[]{:S(2)}) copy-start(bf16[48,6144]{1,0:T(8,128)(2,1)} %param.13) | copy-start | bytes 1769476
  473.1 62.8 %copy-start.2 = (f32[6144]{0:T(1024)S(1)}, f32[6144]{0:T(1024)}, u32[]{:S(2)}) copy-start(f32[6144]{0:T(1024)} %param.15) | copy-start | bytes 73732
Sparse Core Ops, SparseCore 0:
  29.2 181.3 all-gather.1
  473.2 61.3 reduce-scatter.1
